TPU v7x, 512 devices: a whole 4x4x16 slice. The times are simulated.
512 devices in a mesh: grp: 16 (over x, y), clu: 32 (over z, core).
Axes of the slice: x: 4, y: 4, z: 16, core: 2. Of those that a mesh axis runs over, the one named last changes fastest.
Arguments:
- lower_inverse: bfloat16 [32, 2, 512, 512], P('clu', None, 'grp'), as said below
- upper_inverse: bfloat16 [32, 2, 512, 512], P('clu', None, 'grp'), as said below
- lower_factors: bfloat16 [32, 128, 2, 48, 512], P('clu', 'grp'), may hold values from -1.2578125 to 1.2578125
- upper_factors: bfloat16 [32, 128, 2, 48, 512], P('clu', 'grp'), may hold values from -1.2578125 to 1.2578125
- lower_ranks: int32 [32, 128], P('clu', 'grp'), may hold values from 16 to 48
- upper_ranks: int32 [32, 128], P('clu', 'grp'), may hold values from 16 to 48
- pivots: int32 [32, 512], P('clu'), may hold values from 0 to 511, each once within a row
- pair_lower: int32 [32, 512], P('clu', 'grp'), may hold values from 0 to 7
- pair_upper: int32 [32, 512], P('clu', 'grp'), may hold values from 0 to 7
- pair_owner: int32 [32, 512, 1], P('clu', 'grp'), may hold values from 0 to 31; in each aligned block of 32 rows (0 to 31, 32 to 63, ..., all dimensions but the last counted through in order) at most 2 rows name the same one
Outputs:
- lower_solved: bfloat16 [32, 128, 2, 48, 512], P('clu', 'grp')
- upper_solved: bfloat16 [32, 128, 2, 48, 512], P('clu', 'grp')
- arrived: bfloat16 [32, 16, 32, 2, 2, 2304], P('clu', 'grp')
Inputs may be any that keep to these rules, and one draw needn't show every extreme that they name: `lower_inverse`: each cluster's matrix is unit lower triangular: zeros above the diagonal, one on the real part's diagonal and zero on the imaginary part's. `upper_inverse`: each cluster's matrix is upper triangular: zeros below the diagonal in both parts. `pair_owner`: among the 32 pairs of one share, at most 2 name the same owner, and some share reaches it.
All inputs are finite; a program needn't handle non-finite values.
Results may differ from a plain program's by a relative error of at most 0.0058.
Values may be sent and summed in bfloat16 or wider, within the bound.
No kernel may reach another device: no remote copies, remote signals or barrier semaphores. Data moves between devices by JAX's collectives and lax.ppermute only.
A program may use at most 64 MiB of HBM per device.

v0:
```python
import jax
import jax.numpy as jnp
from jax import lax
from jax.sharding import PartitionSpec as P

SEND_CAP = 2


def mask_rows(factors, block_ranks):
    rank_width = factors.shape[2]
    row_index = lax.broadcasted_iota(jnp.int32, (factors.shape[0], rank_width), 1)
    row_mask = row_index < block_ranks[:, None]
    return jnp.where(row_mask[:, None, :, None], factors, jnp.zeros((), factors.dtype))


def product(left, right):
    return jnp.einsum("prb,psb->prs", left, right, preferred_element_type=jnp.float32)


def per_device(
    lower_inverse,
    upper_inverse,
    lower_factors,
    upper_factors,
    lower_ranks,
    upper_ranks,
    pivots,
    pair_lower,
    pair_upper,
    pair_owner,
):
    lower_masked = mask_rows(lower_factors[0], lower_ranks[0])
    upper_masked = mask_rows(upper_factors[0], upper_ranks[0])
    upper_pivoted = jnp.take(upper_masked, pivots[0], axis=3)
    block_count = lower_masked.shape[0]
    rank_width = lower_masked.shape[2]
    panel_count = lower_masked.shape[3]
    lower_real = lower_masked[:, 0].reshape(block_count * rank_width, panel_count)
    lower_imag = lower_masked[:, 1].reshape(block_count * rank_width, panel_count)
    upper_real = upper_pivoted[:, 0].reshape(block_count * rank_width, panel_count)
    upper_imag = upper_pivoted[:, 1].reshape(block_count * rank_width, panel_count)
    contract_last = (((1,), (1,)), ((), ()))
    lower_piece = lax.all_gather(lower_inverse, "grp", axis=2, tiled=True)
    upper_piece = lax.all_gather(upper_inverse, "grp", axis=2, tiled=True)
    piece_real = upper_piece[0, 0]
    piece_imag = upper_piece[0, 1]
    real_part = jnp.dot(lower_real, piece_real, preferred_element_type=jnp.float32) - jnp.dot(
        lower_imag, piece_imag, preferred_element_type=jnp.float32
    )
    imag_part = jnp.dot(lower_real, piece_imag, preferred_element_type=jnp.float32) + jnp.dot(
        lower_imag, piece_real, preferred_element_type=jnp.float32
    )
    lower_totals = jnp.stack([real_part, imag_part], 0)
    piece_real = lower_piece[0, 0]
    piece_imag = lower_piece[0, 1]
    real_part = lax.dot_general(
        upper_real, piece_real, contract_last, preferred_element_type=jnp.float32
    ) - lax.dot_general(upper_imag, piece_imag, contract_last, preferred_element_type=jnp.float32)
    imag_part = lax.dot_general(
        upper_real, piece_imag, contract_last, preferred_element_type=jnp.float32
    ) + lax.dot_general(upper_imag, piece_real, contract_last, preferred_element_type=jnp.float32)
    upper_totals = jnp.stack([real_part, imag_part], 0)
    lower_solved = jnp.transpose(
        lower_totals.astype(jnp.bfloat16).reshape(2, block_count, rank_width, panel_count),
        (1, 0, 2, 3),
    )
    upper_solved = jnp.transpose(
        upper_totals.astype(jnp.bfloat16).reshape(2, block_count, rank_width, panel_count),
        (1, 0, 2, 3),
    )
    left_blocks = lower_solved[pair_lower[0]]
    right_blocks = upper_solved[pair_upper[0]]
    pair_count = left_blocks.shape[0]
    real_part = product(left_blocks[:, 0], right_blocks[:, 0]) - product(
        left_blocks[:, 1], right_blocks[:, 1]
    )
    imag_part = product(left_blocks[:, 0], right_blocks[:, 1]) + product(
        left_blocks[:, 1], right_blocks[:, 0]
    )
    cores = (
        jnp.stack([real_part, imag_part], 1)
        .reshape(pair_count, 2 * rank_width * rank_width)
        .astype(jnp.bfloat16)
    )
    owners = pair_owner[0, :, 0]
    pair_ids = lax.broadcasted_iota(jnp.int32, (pair_count,), 0)
    same_owner = (owners[:, None] == owners[None, :]) & (pair_ids[None, :] < pair_ids[:, None])
    slots = jnp.sum(same_owner.astype(jnp.int32), axis=1)
    clusters = lax.axis_size("clu")
    target_slot = owners * SEND_CAP + slots
    slot_ids = lax.broadcasted_iota(jnp.int32, (clusters * SEND_CAP, pair_count), 0)
    one_hot = (slot_ids == target_slot[None, :]).astype(jnp.bfloat16)
    buffer = jnp.dot(one_hot, cores, preferred_element_type=jnp.float32).astype(jnp.bfloat16)
    buffer = buffer.reshape(clusters, SEND_CAP, 2, rank_width * rank_width)
    arrived = lax.all_to_all(buffer, "clu", split_axis=0, concat_axis=0, tiled=True)
    return (lower_solved[None], upper_solved[None], arrived[None, None])


def solution(mesh):
    in_specs = (
        P("clu", None, "grp", None),
        P("clu", None, "grp", None),
        P("clu", "grp", None, None, None),
        P("clu", "grp", None, None, None),
        P("clu", "grp"),
        P("clu", "grp"),
        P("clu", None),
        P("clu", "grp"),
        P("clu", "grp"),
        P("clu", "grp", None),
    )
    out_specs = (
        P("clu", "grp", None, None, None),
        P("clu", "grp", None, None, None),
        P("clu", "grp", None, None, None, None),
    )
    return jax.shard_map(
        per_device, mesh=mesh, in_specs=in_specs, out_specs=out_specs, check_vma=False
    )
```

profile of v0, /device:TPU:1, one launch (start us, length us, event | category | flops | bytes accessed | tf_op | source)
XLA Modules:
  0.0 210.7 jit_solution(4374763556248300210)
XLA Ops:
  8.7 2.6 %copy.48 = bf16[1,8,2,48,512]{3,1,4,2,0:T(8,128)(2,1)S(1)} copy(bf16[1,8,2,48,512]{4,3,2,1,0:T(8,128)(2,1)} %param.13) | data formatting | bytes 1572864 | tf_op args[3]
  11.4 2.5 %copy.43 = bf16[1,8,2,48,512]{3,1,4,2,0:T(8,128)(2,1)} copy(bf16[1,8,2,48,512]{4,3,2,1,0:T(8,128)(2,1)S(1)} %copy-done.8) | data formatting | bytes 1572864 | tf_op args[2]
  14.0 1.4 bitcast_select_fusion
  15.4 3.0 %gather_fusion = bf16[512,8,2,48]{3,1,2,0:T(8,128)(2,1)S(1)} fusion(bf16[8,2,48,512]{2,0,3,1:T(8,128)(2,1)} %bitcast_select_fusion, s32[1024]{0:T(1024)S(1)} %pad_clamp_fusion.2), kind=kCustom, calls=%fused_computation | custom fusion | bytes 1574912 | tf_op jit(solution)/shard_map/jit(_take)/gather | solution.py:34
  18.4 1.8 select_bitcast_fusion
  20.3 1.1 fusion.26
  21.4 2.6 %copy.49 = bf16[8,1,48,512]{3,2,0,1:T(8,128)(2,1)} copy(bf16[8,1,48,512]{2,0,1,3:T(8,128)(2,1)} %get-tuple-element.4) | data formatting | bytes 786432 | tf_op jit(solution)/shard_map/slice | solution.py:40
  24.0 0.7 copy.50
  24.8 1.1 fusion.27
  25.9 2.7 %copy.44 = bf16[8,1,48,512]{3,2,0,1:T(8,128)(2,1)} copy(bf16[8,1,48,512]{2,0,3,1:T(8,128)(2,1)} %get-tuple-element.6) | data formatting | bytes 786432 | tf_op jit(solution)/shard_map/slice | solution.py:38
  29.5 42.9 %all-gather.5.cloned.1.call-done = bf16[1,2,512,512]{3,2,1,0:T(8,128)(2,1)} async-done(((bf16[1,2,32,512]{3,2,1,0:T(8,128)(2,1)}), bf16[1,2,512,512]{3,2,1,0:T(8,128)(2,1)}) %all-gather.5.cloned.1.call-update) | async-done | bytes 1048592 | tf_op jit(solution)/shard_map/all_gather | solution.py:43
  72.4 2.3 %fusion.21 = f32[384,512]{1,0:T(8,128)} fusion(bf16[384,512]{1,0:T(8,128)(2,1)S(1)} %bitcast.132, bf16[1,2,512,512]{3,2,1,0:T(8,128)(2,1)} %all-gather.5.cloned.1.call-done), kind=kOutput, calls=%fused_computation.43 | convolution fusion | flops 201326592 | bytes 1703936 | tf_op jit(solution)/shard_map/dot_general | solution.py:59
  74.7 1.4 fusion.20
  76.2 56.5 %all-gather.3.cloned.1.call-done = bf16[1,2,512,512]{3,2,1,0:T(8,128)(2,1)} async-done(((bf16[1,2,32,512]{3,2,1,0:T(8,128)(2,1)}), bf16[1,2,512,512]{3,2,1,0:T(8,128)(2,1)}) %all-gather.3.cloned.1.call-update) | async-done | bytes 1048592 | tf_op jit(solution)/shard_map/all_gather | solution.py:44
  132.7 1.5 fusion.19
  134.2 1.4 fusion.18
  137.6 1.3 fusion.15
  138.9 2.4 %gather_fusion.1 = bf16[32,2,48,512]{3,2,1,0:T(8,128)(2,1)} fusion(bf16[8,2,48,512]{3,2,1,0:T(8,128)(2,1)S(1)} %get-tuple-element.12, s32[1024]{0:T(1024)S(1)} %pad_clamp_fusion.1), kind=kCustom, calls=%fused_computation.1 | custom fusion | bytes 6291584 | tf_op jit(solution)/shard_map/gather | solution.py:71
  141.3 2.4 %gather_fusion.2 = bf16[32,2,48,512]{3,2,1,0:T(8,128)(2,1)} fusion(bf16[8,2,48,512]{3,2,1,0:T(8,128)(2,1)S(1)} %get-tuple-element.7, s32[1024]{0:T(1024)S(1)} %pad_clamp_fusion), kind=kCustom, calls=%fused_computation.2 | custom fusion | bytes 6291584 | tf_op jit(solution)/shard_map/gather | solution.py:72
  143.8 2.6 %fusion = f32[32,48,48]{2,1,0:T(8,128)S(1)} fusion(bf16[32,2,48,512]{3,2,1,0:T(8,128)(2,1)} %gather_fusion.1, bf16[32,2,48,512]{3,2,1,0:T(8,128)(2,1)} %gather_fusion.2), kind=kOutput, calls=%fused_computation.11 | convolution fusion | flops 75497472 | bytes 3440640 | tf_op jit(solution)/shard_map/prb,psb->prs/dot_general | solution.py:17
  146.6 2.1 fusion.1
  150.3 1.4 convert_element_type.16
  152.2 50.9 %all_to_all.5 = bf16[32,2,2,2304]{3,2,1,0:T(2,128)(2,1)S(1)} all-to-all(bf16[32,2,2,2304]{3,2,1,0:T(2,128)(2,1)S(1)} %reshape.167), channel_id=1, replica_groups=mesh['grp'=16,'clu'=32] {'clu'}, dimensions={0} | all-to-all | bytes 1179648 | tf_op jit(solution)/shard_map/all_to_all | solution.py:95
  203.0 0.8 copy.63
  (57 shorter events, 7.0 us)
Async XLA Ops:
  7.2 4.1 %copy-start.10 = (s32[1,8]{1,0:T(1,128)S(1)}, s32[1,8]{1,0:T(1,128)}, u32[]{:S(2)}) copy-start(s32[1,8]{1,0:T(1,128)} %param.15) | copy-start | bytes 100
  7.2 4.2 %copy-start.9 = (s32[1,512]{1,0:T(1,128)S(1)}, s32[1,512]{1,0:T(1,128)}, u32[]{:S(2)}) copy-start(s32[1,512]{1,0:T(1,128)} %param.16) | copy-start | bytes 6148
  7.2 4.2 %copy-start.8 = (bf16[1,8,2,48,512]{4,3,2,1,0:T(8,128)(2,1)S(1)}, bf16[1,8,2,48,512]{4,3,2,1,0:T(8,128)(2,1)}, u32[]{:S(2)}) copy-start(bf16[1,8,2,48,512]{4,3,2,1,0:T(8,128)(2,1)} %param.12) | copy-start | bytes 2359300
  7.2 65.2 %all-gather.5.cloned.1.call-start = ((), (), s32[]{:S(2)}) async-start(), calls=%async_computation.2 | async-start | bytes 1114112 | tf_op jit(solution)/shard_map/all_gather | solution.py:43
  7.9 124.8 %all-gather.3.cloned.1.call-start = ((), (), s32[]{:S(2)}) async-start(), calls=%async_computation.1 | async-start | bytes 1114112 | tf_op jit(solution)/shard_map/all_gather | solution.py:44
  11.3 2.6 %copy-start.11 = (s32[1,8]{1,0:T(1,128)S(1)}, s32[1,8]{1,0:T(1,128)}, u32[]{:S(2)}) copy-start(s32[1,8]{1,0:T(1,128)} %param.14) | copy-start | bytes 100
  18.4 1.8 copy-start
  25.9 3.4 %copy-start.12 = (s32[1,32]{1,0:T(1,128)S(1)}, s32[1,32]{1,0:T(1,128)}, u32[]{:S(2)}) copy-start(s32[1,32]{1,0:T(1,128)} %param.17) | copy-start | bytes 388
  25.9 3.4 %copy-start.13 = (s32[1,32]{1,0:T(1,128)S(1)}, s32[1,32]{1,0:T(1,128)}, u32[]{:S(2)}) copy-start(s32[1,32]{1,0:T(1,128)} %param.18) | copy-start | bytes 388
  25.9 3.5 %copy-start.14 = (s32[1,32,1]{1,2,0:T(1,128)S(1)}, s32[1,32,1]{1,2,0:T(1,128)}, u32[]{:S(2)}) copy-start(s32[1,32,1]{1,2,0:T(1,128)} %param.19) | copy-start | bytes 388
  25.9 46.5 %copy-start.3 = (bf16[8,1,48,512]{3,2,0,1:T(8,128)(2,1)S(1)}, bf16[8,1,48,512]{3,2,0,1:T(8,128)(2,1)}, u32[]{:S(2)}) copy-start(bf16[8,1,48,512]{3,2,0,1:T(8,128)(2,1)} %copy.49) | copy-start | bytes 1179652
  29.3 103.4 %copy-start.4 = (bf16[8,1,48,512]{3,2,0,1:T(8,128)(2,1)S(1)}, bf16[8,1,48,512]{3,2,0,1:T(8,128)(2,1)}, u32[]{:S(2)}) copy-start(bf16[8,1,48,512]{3,2,0,1:T(8,128)(2,1)} %copy.44) | copy-start | bytes 1179652
  76.2 59.4 %copy-start.1 = (bf16[1,2,512,512]{3,2,1,0:T(8,128)(2,1)S(1)}, bf16[1,2,512,512]{3,2,1,0:T(8,128)(2,1)}, u32[]{:S(2)}) copy-start(bf16[1,2,512,512]{3,2,1,0:T(8,128)(2,1)} %all-gather.5.cloned.1.call-done) | copy-start | bytes 3145732
  132.7 2.9 %copy-start.7 = (f32[384,512]{1,0:T(8,128)S(1)}, f32[384,512]{1,0:T(8,128)}, u32[]{:S(2)}) copy-start(f32[384,512]{1,0:T(8,128)} %fusion.21) | copy-start | bytes 2359300
  135.6 1.2 copy-start.2
  143.8 2.8 %copy-start.5 = (bf16[32,2,48,512]{3,2,1,0:T(8,128)(2,1)S(1)}, bf16[32,2,48,512]{3,2,1,0:T(8,128)(2,1)}, u32[]{:S(2)}) copy-start(bf16[32,2,48,512]{3,2,1,0:T(8,128)(2,1)} %gather_fusion.1) | copy-start | bytes 9437188
  146.6 2.4 %copy-start.6 = (bf16[32,2,48,512]{3,2,1,0:T(8,128)(2,1)S(1)}, bf16[32,2,48,512]{3,2,1,0:T(8,128)(2,1)}, u32[]{:S(2)}) copy-start(bf16[32,2,48,512]{3,2,1,0:T(8,128)(2,1)} %gather_fusion.2) | copy-start | bytes 9437188
Sparse Core Ops, SparseCore 0:
  11.1 61.2 all-gather.4
  75.5 57.1 all-gather.2
where the time goes:
time: 211 us
  waiting for transfers between devices  101 us (48%)
  blocking collectives  50.9 us (24%)
  local copies, waits for them, and re-layouts  25.2 us (12%)
  between operations  14.4 us (7%)
  matrix products  14.2 us (7%)
  other arithmetic  5.23 us (2%)
    all_gather x1, waiting for transfers between devices, per_device(): upper_piece = lax.all_gather(upper_inverse, 'grp', axis=2, tiled=True)  56.5 us
    all_to_all x1, blocking collectives, per_device(): lax.all_to_all(buffer, 'clu', split_axis=0, concat_axis=0, tiled=True)  50.9 us
    all_gather x1, waiting for transfers between devices, per_device(): lower_piece = lax.all_gather(lower_inverse, 'grp', axis=2, tiled=True)  42.9 us
    unnamed x33, local copies, waits for them, and re-layouts  6.88 us
    dot_general x4, matrix products, product(): jnp.einsum('prb,psb->prs', left, right, preferred_element_type=jnp.float32)  5.78 us
  transfers between devices with their start and end apart: 2, of which 2 were waited for; matrix products, arithmetic and copies ran while one was open for 12% of the time, Pallas kernels for 0%

commit v1 on v0

--- a/solution.py
+++ b/solution.py
@@ -40,7 +40,9 @@
     upper_real = upper_pivoted[:, 0].reshape(block_count * rank_width, panel_count)
     upper_imag = upper_pivoted[:, 1].reshape(block_count * rank_width, panel_count)
     contract_last = (((1,), (1,)), ((), ()))
-    lower_piece = lax.all_gather(lower_inverse, "grp", axis=2, tiled=True)
+    lower_piece = jnp.concatenate(
+        lax.all_to_all(jnp.stack([lower_inverse] * lax.axis_size("grp")), "grp", 0, 0), axis=2
+    )
     upper_piece = lax.all_gather(upper_inverse, "grp", axis=2, tiled=True)
     piece_real = upper_piece[0, 0]
     piece_imag = upper_piece[0, 1]

time: 211 us -> 159 us (0.75)
  waiting for transfers between devices: 101 us -> 41.8 us
  starting transfers between devices: 0.08 us -> 7.75 us
  matrix products: 14.2 us -> 12 us
    all_gather x1 -> x0, waiting for transfers between devices: 42.9 us -> none  [per_device(): lower_piece = lax.all_gather(lower_inverse, 'grp', axis=2, tiled=True)]
    all_gather x1, waiting for transfers between devices: 56.5 us -> 41.1 us  [per_device(): upper_piece = lax.all_gather(upper_inverse, 'grp', axis=2, tiled=True)]
    all_to_all x0 -> x1, starting transfers between devices: none -> 7.7 us  [per_device(): lax.all_to_all(jnp.stack([lower_inverse] * lax.axis_size('grp')), 'grp',...]
    unnamed x33 -> x31, local copies, waits for them, and re-layouts: 6.88 us -> 7.54 us
  transfers between devices with their start and end apart: 2 -> 2, of which waited for: 2 -> 1; matrix products, arithmetic and copies ran while one was open for 12% -> 14% of each run, Pallas kernels for 0% -> 0%
where the time goes in v1:
time: 159 us
  blocking collectives  50.9 us (32%)
  waiting for transfers between devices  41.8 us (26%)
  local copies, waits for them, and re-layouts  26.7 us (17%)
  between operations  14.3 us (9%)
  matrix products  12 us (8%)
  starting transfers between devices  7.75 us (5%)
  other arithmetic  5.27 us (3%)
    all_to_all x1, blocking collectives, per_device(): lax.all_to_all(buffer, 'clu', split_axis=0, concat_axis=0, tiled=True)  50.9 us
    all_gather x1, waiting for transfers between devices, per_device(): upper_piece = lax.all_gather(upper_inverse, 'grp', axis=2, tiled=True)  41.1 us
    all_to_all x1, starting transfers between devices, per_device(): lax.all_to_all(jnp.stack([lower_inverse] * lax.axis_size('grp')), 'grp',...  7.7 us
    unnamed x31, local copies, waits for them, and re-layouts  7.54 us
    dot_general x4, matrix products, product(): jnp.einsum('prb,psb->prs', left, right, preferred_element_type=jnp.float32)  5.78 us
  transfers between devices with their start and end apart: 2, of which 1 were waited for; matrix products, arithmetic and copies ran while one was open for 14% of the time, Pallas kernels for 0%

profile of v1, /device:TPU:1, one launch (start us, length us, event | category | flops | bytes accessed | tf_op | source)
XLA Modules:
  0.0 158.7 jit_solution(6042817532090530285)
XLA Ops:
  7.2 2.0 %stack.52 = bf16[16,1,2,32,512]{4,3,2,1,0:T(8,128)(2,1)} broadcast(bf16[2,32,512]{2,1,0:T(8,128)(2,1)} %bitcast.149), dimensions={2,3,4} | broadcast | bytes 1114112 | tf_op jit(solution)/shard_map/stack | solution.py:44
  9.1 7.7 %all-to-all-start = ((bf16[16,1,2,32,512]{4,3,2,1,0:T(8,128)(2,1)}), bf16[16,1,2,32,512]{4,3,2,1,0:T(8,128)(2,1)S(1)}, u32[]{:S(2)}, u32[]{:S(2)}) async-start(bf16[16,1,2,32,512]{4,3,2,1,0:T(8,128)(2,1)} %stack.52), calls=%async_computation | async-start | bytes 2097152 | tf_op jit(solution)/shard_map/all_to_all | solution.py:44
  17.6 2.6 %copy.64 = bf16[1,8,2,48,512]{3,1,4,2,0:T(8,128)(2,1)S(1)} copy(bf16[1,8,2,48,512]{4,3,2,1,0:T(8,128)(2,1)} %param.13) | data formatting | bytes 1572864 | tf_op args[3]
  20.3 1.5 bitcast_select_fusion
  21.8 3.0 %gather_fusion = bf16[512,8,2,48]{3,1,2,0:T(8,128)(2,1)S(1)} fusion(bf16[8,2,48,512]{2,0,3,1:T(8,128)(2,1)} %bitcast_select_fusion, s32[1024]{0:T(1024)S(1)} %pad_clamp_fusion.2), kind=kCustom, calls=%fused_computation | custom fusion | bytes 1574912 | tf_op jit(solution)/shard_map/jit(_take)/gather | solution.py:34
  24.7 1.8 %select_bitcast_fusion = bf16[8,2,48,512]{2,0,1,3:T(8,128)(2,1)S(1)} fusion(bf16[512,8,2,48]{3,1,2,0:T(8,128)(2,1)S(1)} %gather_fusion, pred[512]{0:T(512)(128)(4,1)S(1)} %compare_and_fusion), kind=kLoop, calls=%fused_computation.6 | loop fusion | flops 393216 | bytes 1573376 | tf_op jit(solution)/shard_map/jit(_take)/select_n | solution.py:34
  26.5 1.5 fusion.26
  28.0 2.6 %copy.59 = bf16[1,8,2,48,512]{3,1,4,2,0:T(8,128)(2,1)S(1)} copy(bf16[1,8,2,48,512]{4,3,2,1,0:T(8,128)(2,1)} %param.12) | data formatting | bytes 1572864 | tf_op args[2]
  30.9 1.5 fusion.27
  32.4 1.5 copy.65
  33.9 0.7 copy.67
  34.7 1.9 %copy.60 = bf16[8,1,48,512]{3,2,0,1:T(8,128)(2,1)S(1)} copy(bf16[8,1,48,512]{2,0,3,1:T(8,128)(2,1)} %get-tuple-element.6) | data formatting | bytes 786432 | tf_op jit(solution)/shard_map/slice | solution.py:38
  39.4 1.1 fusion.8
  40.6 41.1 %all-gather.2.cloned.1.call-done = bf16[1,2,512,512]{3,2,1,0:T(8,128)(2,1)} async-done(((bf16[1,2,32,512]{3,2,1,0:T(8,128)(2,1)}), bf16[1,2,512,512]{3,2,1,0:T(8,128)(2,1)}) %all-gather.2.cloned.1.call-update) | async-done | bytes 1048592 | tf_op jit(solution)/shard_map/all_gather | solution.py:46
  81.7 1.5 fusion.19
  83.2 1.4 fusion.18
  85.6 1.3 fusion.15
  87.0 2.4 %gather_fusion.1 = bf16[32,2,48,512]{3,2,1,0:T(8,128)(2,1)} fusion(bf16[8,2,48,512]{3,2,1,0:T(8,128)(2,1)S(1)} %get-tuple-element.12, s32[1024]{0:T(1024)S(1)} %pad_clamp_fusion.1), kind=kCustom, calls=%fused_computation.1 | custom fusion | bytes 6291584 | tf_op jit(solution)/shard_map/gather | solution.py:73
  89.3 2.4 %gather_fusion.2 = bf16[32,2,48,512]{3,2,1,0:T(8,128)(2,1)} fusion(bf16[8,2,48,512]{3,2,1,0:T(8,128)(2,1)S(1)} %get-tuple-element.7, s32[1024]{0:T(1024)S(1)} %pad_clamp_fusion), kind=kCustom, calls=%fused_computation.2 | custom fusion | bytes 6291584 | tf_op jit(solution)/shard_map/gather | solution.py:74
  91.8 2.6 %fusion = f32[32,48,48]{2,1,0:T(8,128)S(1)} fusion(bf16[32,2,48,512]{3,2,1,0:T(8,128)(2,1)} %gather_fusion.1, bf16[32,2,48,512]{3,2,1,0:T(8,128)(2,1)} %gather_fusion.2), kind=kOutput, calls=%fused_computation.11 | convolution fusion | flops 75497472 | bytes 3440640 | tf_op jit(solution)/shard_map/prb,psb->prs/dot_general | solution.py:17
  94.6 2.1 %fusion.1 = f32[32,48,48]{2,1,0:T(8,128)S(1)} fusion(bf16[32,2,48,512]{3,2,1,0:T(8,128)(2,1)S(1)} %copy-done.5, bf16[32,2,48,512]{3,2,1,0:T(8,128)(2,1)} %gather_fusion.2), kind=kOutput, calls=%fused_computation.12 | convolution fusion | flops 75497472 | bytes 3440640 | tf_op jit(solution)/shard_map/prb,psb->prs/dot_general | solution.py:17
  98.3 1.4 convert_element_type.16
  100.2 50.9 %all_to_all.10 = bf16[32,2,2,2304]{3,2,1,0:T(2,128)(2,1)S(1)} all-to-all(bf16[32,2,2,2304]{3,2,1,0:T(2,128)(2,1)S(1)} %reshape.178), channel_id=1, replica_groups=mesh['grp'=16,'clu'=32] {'clu'}, dimensions={0} | all-to-all | bytes 1179648 | tf_op jit(solution)/shard_map/all_to_all | solution.py:97
  151.0 0.8 copy.80
  (56 shorter events, 7.3 us)
Async XLA Ops:
  9.1 11.1 %copy-start.9 = (s32[1,8]{1,0:T(1,128)S(1)}, s32[1,8]{1,0:T(1,128)}, u32[]{:S(2)}) copy-start(s32[1,8]{1,0:T(1,128)} %param.15) | copy-start | bytes 100
  9.1 11.1 %copy-start.8 = (s32[1,512]{1,0:T(1,128)S(1)}, s32[1,512]{1,0:T(1,128)}, u32[]{:S(2)}) copy-start(s32[1,512]{1,0:T(1,128)} %param.16) | copy-start | bytes 6148
  9.1 28.4 %all-to-all-start = ((bf16[16,1,2,32,512]{4,3,2,1,0:T(8,128)(2,1)}), bf16[16,1,2,32,512]{4,3,2,1,0:T(8,128)(2,1)S(1)}, u32[]{:S(2)}, u32[]{:S(2)}) async-start(bf16[16,1,2,32,512]{4,3,2,1,0:T(8,128)(2,1)} %stack.52), calls=%async_computation | async-start | bytes 2097152 | tf_op jit(solution)/shard_map/all_to_all | solution.py:44
  16.8 64.9 %all-gather.2.cloned.1.call-start = ((), (), s32[]{:S(2)}) async-start(), calls=%async_computation.2 | async-start | bytes 1114112 | tf_op jit(solution)/shard_map/all_gather | solution.py:46
  28.0 2.6 %copy-start.10 = (s32[1,8]{1,0:T(1,128)S(1)}, s32[1,8]{1,0:T(1,128)}, u32[]{:S(2)}) copy-start(s32[1,8]{1,0:T(1,128)} %param.14) | copy-start | bytes 100
  30.8 1.5 copy-start.11
  30.8 1.6 %copy-start.2 = (bf16[8,1,48,512]{2,0,1,3:T(8,128)(2,1)S(1)}, bf16[8,1,48,512]{2,0,1,3:T(8,128)(2,1)}, u32[]{:S(2)}) copy-start(bf16[8,1,48,512]{2,0,1,3:T(8,128)(2,1)} %get-tuple-element.4) | copy-start | bytes 1179652
  30.8 3.1 %copy-start.1 = (bf16[8,1,48,512]{2,0,1,3:T(8,128)(2,1)S(1)}, bf16[8,1,48,512]{2,0,1,3:T(8,128)(2,1)}, u32[]{:S(2)}) copy-start(bf16[8,1,48,512]{2,0,1,3:T(8,128)(2,1)} %get-tuple-element.3) | copy-start | bytes 1179652
  33.9 2.6 %copy-start.3 = (bf16[8,1,48,512]{2,0,3,1:T(8,128)(2,1)S(1)}, bf16[8,1,48,512]{2,0,3,1:T(8,128)(2,1)}, u32[]{:S(2)}) copy-start(bf16[8,1,48,512]{2,0,3,1:T(8,128)(2,1)} %get-tuple-element.5) | copy-start | bytes 1179652
  33.9 3.4 %copy-start.12 = (s32[1,32]{1,0:T(1,128)S(1)}, s32[1,32]{1,0:T(1,128)}, u32[]{:S(2)}) copy-start(s32[1,32]{1,0:T(1,128)} %param.18) | copy-start | bytes 388
  33.9 3.4 %copy-start.13 = (s32[1,32,1]{1,2,0:T(1,128)S(1)}, s32[1,32,1]{1,2,0:T(1,128)}, u32[]{:S(2)}) copy-start(s32[1,32,1]{1,2,0:T(1,128)} %param.19) | copy-start | bytes 388
  37.2 1.0 copy-start.4
  81.7 2.9 %copy-start = (bf16[1,2,512,512]{3,2,1,0:T(8,128)(2,1)S(1)}, bf16[1,2,512,512]{3,2,1,0:T(8,128)(2,1)}, u32[]{:S(2)}) copy-start(bf16[1,2,512,512]{3,2,1,0:T(8,128)(2,1)} %all-gather.2.cloned.1.call-done) | copy-start | bytes 3145732
  84.6 1.0 copy-start.7
  91.8 2.8 %copy-start.5 = (bf16[32,2,48,512]{3,2,1,0:T(8,128)(2,1)S(1)}, bf16[32,2,48,512]{3,2,1,0:T(8,128)(2,1)}, u32[]{:S(2)}) copy-start(bf16[32,2,48,512]{3,2,1,0:T(8,128)(2,1)} %gather_fusion.1) | copy-start | bytes 9437188
  94.6 2.4 %copy-start.6 = (bf16[32,2,48,512]{3,2,1,0:T(8,128)(2,1)S(1)}, bf16[32,2,48,512]{3,2,1,0:T(8,128)(2,1)}, u32[]{:S(2)}) copy-start(bf16[32,2,48,512]{3,2,1,0:T(8,128)(2,1)} %gather_fusion.2) | copy-start | bytes 9437188
Sparse Core Ops, SparseCore 0:
  20.7 60.9 all-gather.1
